TPU v7x, 256 devices: a whole 4x4x8 slice. The times are simulated.
256 devices in a mesh: req: 32 (over x, y, core), tp: 8 (over z).
Axes of the slice: x: 4, y: 4, z: 8, core: 2. Of those that a mesh axis runs over, the one named last changes fastest.
Arguments:
- query: bfloat16 [768, 4096], P('req', 'tp'), may hold values from -102 to 102
- new_key: bfloat16 [768, 1024], P('req', 'tp'), may hold values from -6 to 6
- new_value: bfloat16 [768, 1024], P('req', 'tp'), may hold values from -6 to 6
- prefix_key: bfloat16 [64, 6144, 1024], P('req', None, 'tp'), may hold values from -6 to 6
- prefix_value: bfloat16 [64, 6144, 1024], P('req', None, 'tp'), may hold values from -6 to 6
- suffix_key: bfloat16 [768, 128, 1024], P('req', None, 'tp'), may hold values from -6 to 6
- suffix_value: bfloat16 [768, 128, 1024], P('req', None, 'tp'), may hold values from -6 to 6
- group_ids: int32 [768], replicated, may hold values from 0 to 63, as said below
- prompt_len: int32 [64], P('req'), may hold values from 768 to 6144, as said below
- suffix_len: int32 [768], replicated, may hold values from 1 to 128, as said below
- o_weight: bfloat16 [4096, 4096], P('tp'), may hold values from -0.09375 to 0.09375
- residual: bfloat16 [768, 4096], P('req'), may hold values from -0.29882812 to 0.29882812
- norm_gain: bfloat16 [4096], replicated, may hold values from 0.5 to 1.5
Outputs:
- hidden: bfloat16 [768, 4096], P('req')
- normed: bfloat16 [768, 4096], P('req')
Inputs may be any that keep to these rules, and one draw needn't show every extreme that they name: Request r belongs to group group_ids[r]; groups 2k to 2k + 1 at a time are held together (group // 2 names the holder). Among each aligned block of 24 requests, every holder that appears is named by exactly 2 of them. `prompt_len`: some group has exactly 6144. `suffix_len`: some request has exactly 128.
All inputs are finite; a program needn't handle non-finite values.
Results may differ from a plain program's by a relative error of at most 0.008.
Values may be sent and summed in bfloat16 or wider, within the bound.
No kernel may reach another device: no remote copies, remote signals or barrier semaphores. Data moves between devices by JAX's collectives and lax.ppermute only.
A program may use at most 64 MiB of HBM per device.

v0:
```python
import math
import jax
import jax.numpy as jnp
from jax import lax
from jax.sharding import PartitionSpec as P

HD = 128
WIN = 4096
SINKS = 4
FAR_BELOW = -1e30
NORM_EPS = 1e-06


def prefix_attend(
    rows_query, row_group, row_suffix, prefix_key, prefix_value, prompt_len, first_group, blocks
):
    row_count = rows_query.shape[0]
    groups_dev = prefix_key.shape[0]
    prompt_max = prefix_key.shape[1]
    kv_dev = prefix_key.shape[2] // HD
    heads_dev = rows_query.shape[1] // HD
    repeat = heads_dev // kv_dev
    block_len = min(512, prompt_max)
    score_scale = 1.0 / math.sqrt(HD)
    local_group = row_group - first_group
    owned = (local_group >= 0) & (local_group < groups_dev)
    member = local_group[:, None] == jnp.arange(groups_dev, dtype=jnp.int32)[None, :]
    row_prompt = jnp.sum(jnp.where(member, prompt_len[None, :], 0), axis=1)
    row_low = row_prompt + row_suffix - WIN + 1
    queries = rows_query.reshape(row_count, kv_dev, repeat, HD)

    def key_step(block_index, loop_state):
        running, weight_sum, weighted = loop_state
        key_start = block_index * block_len
        key_block = lax.dynamic_slice_in_dim(prefix_key, key_start, block_len, 1).reshape(
            groups_dev, block_len, kv_dev, HD
        )
        value_block = lax.dynamic_slice_in_dim(prefix_value, key_start, block_len, 1).reshape(
            groups_dev, block_len, kv_dev, HD
        )
        scores = (
            jnp.einsum("rkhd,gpkd->rkhgp", queries, key_block, preferred_element_type=jnp.float32)
            * score_scale
        )
        positions = key_start + jnp.arange(block_len, dtype=jnp.int32)
        inside = positions[None, :] < prompt_len[:, None]
        window = (positions[None, :] < SINKS) | (positions[None, :] >= row_low[:, None])
        usable = member[:, :, None] & inside[None, :, :] & window[:, None, :]
        usable = usable[:, None, None, :, :]
        masked = jnp.where(usable, scores, FAR_BELOW)
        updated = jnp.maximum(running, jnp.max(masked, axis=(3, 4)))
        weights = jnp.where(usable, jnp.exp(masked - updated[..., None, None]), 0.0)
        rescale = jnp.exp(running - updated)
        weight_sum = weight_sum * rescale + jnp.sum(weights, axis=(3, 4))
        rounded = weights.astype(jnp.bfloat16)
        weighted = weighted * rescale[..., None] + jnp.einsum(
            "rkhgp,gpkd->rkhd", rounded, value_block, preferred_element_type=jnp.float32
        )
        return (updated, weight_sum, weighted)

    initial = (
        jnp.full((row_count, kv_dev, repeat), FAR_BELOW, jnp.float32),
        jnp.zeros((row_count, kv_dev, repeat), jnp.float32),
        jnp.zeros((row_count, kv_dev, repeat, HD), jnp.float32),
    )
    running, weight_sum, weighted = lax.fori_loop(0, blocks, key_step, initial)
    bounded = jnp.maximum(weight_sum, 1.0)
    normalized = jnp.where(owned[:, None, None, None], weighted / bounded[..., None], 0.0).reshape(
        row_count, heads_dev * HD
    )
    log_total = jnp.where(owned[:, None, None], running + jnp.log(bounded), 0.0).reshape(
        row_count, heads_dev
    )
    return (normalized, log_total)


def body(
    query,
    new_key,
    new_value,
    prefix_key,
    prefix_value,
    suffix_key,
    suffix_value,
    group_ids,
    prompt_len,
    suffix_len,
    o_weight,
    residual,
    norm_gain,
):
    req_dev = query.shape[0]
    heads_dev = query.shape[1] // HD
    kv_dev = new_key.shape[1] // HD
    repeat = heads_dev // kv_dev
    groups_dev = prefix_key.shape[0]
    prompt_max = prefix_key.shape[1]
    suffix_max = suffix_key.shape[1]
    block_len = min(512, prompt_max)
    score_scale = 1.0 / math.sqrt(HD)
    places = lax.axis_size("req")
    device = lax.axis_index("req")
    first_group = device * groups_dev
    own_suffix = lax.dynamic_slice_in_dim(suffix_len, device * req_dev, req_dev)
    blocks = prompt_max // block_len
    capacity = max(2, req_dev // places)
    slot_total = places * capacity
    all_groups = group_ids.reshape(places, 1, req_dev)
    all_suffix = suffix_len.reshape(places, 1, req_dev)
    all_rows = (
        jnp.arange(places, dtype=jnp.int32)[:, None] * req_dev
        + jnp.arange(req_dev, dtype=jnp.int32)[None, :]
    ).reshape(places, 1, req_dev)
    is_mine = (group_ids // groups_dev).reshape(places, req_dev) == device
    slot_order = jnp.cumsum(is_mine.astype(jnp.int32), axis=1) - 1
    slot_pick = is_mine[:, None, :] & (
        slot_order[:, None, :] == jnp.arange(capacity, dtype=jnp.int32)[None, :, None]
    )
    filled = jnp.any(slot_pick, axis=2)
    slot_group = jnp.where(
        filled, jnp.sum(jnp.where(slot_pick, all_groups, 0), axis=2), -1
    ).reshape(slot_total)
    slot_suffix = jnp.sum(jnp.where(slot_pick, all_suffix, 0), axis=2).reshape(slot_total)
    slot_row = jnp.where(filled, jnp.sum(jnp.where(slot_pick, all_rows, 0), axis=2), -1).reshape(
        slot_total
    )
    every_query = lax.all_gather(query, "req", axis=0, tiled=True)
    pick_rows = slot_row[:, None] == jnp.arange(places * req_dev, dtype=jnp.int32)[None, :]
    compact = jnp.dot(
        pick_rows.astype(jnp.bfloat16), every_query, preferred_element_type=jnp.float32
    ).astype(jnp.bfloat16)
    part_out, part_log = prefix_attend(
        compact, slot_group, slot_suffix, prefix_key, prefix_value, prompt_len, first_group, blocks
    )
    spread_rows = pick_rows.T.astype(jnp.float32)
    spread_out = jnp.dot(spread_rows, part_out, precision=lax.Precision.HIGHEST)
    spread_log = jnp.dot(spread_rows, part_log, precision=lax.Precision.HIGHEST)
    prefix_out, prefix_log = (
        lax.psum_scatter(spread_out, "req", scatter_dimension=0, tiled=True),
        lax.psum_scatter(spread_log, "req", scatter_dimension=0, tiled=True),
    )
    queries = query.reshape(req_dev, kv_dev, repeat, HD)
    key_rows = suffix_key.reshape(req_dev, suffix_max, kv_dev, HD)
    value_rows = suffix_value.reshape(req_dev, suffix_max, kv_dev, HD)
    scores = (
        jnp.einsum("rkhd,rjkd->rkhj", queries, key_rows, preferred_element_type=jnp.float32)
        * score_scale
    )
    own_score = (
        jnp.einsum(
            "rkhd,rkd->rkh",
            queries,
            new_key.reshape(req_dev, kv_dev, HD),
            preferred_element_type=jnp.float32,
        )
        * score_scale
    )
    usable = (jnp.arange(suffix_max, dtype=jnp.int32)[None, :] < own_suffix[:, None])[
        :, None, None, :
    ]
    masked = jnp.where(usable, scores, FAR_BELOW)
    running = jnp.maximum(jnp.max(masked, axis=-1), own_score)
    weights = jnp.where(usable, jnp.exp(masked - running[..., None]), 0.0)
    own_weight = jnp.exp(own_score - running)
    weight_sum = jnp.sum(weights, axis=-1) + own_weight
    weighted = jnp.einsum(
        "rkhj,rjkd->rkhd",
        weights.astype(jnp.bfloat16),
        value_rows,
        preferred_element_type=jnp.float32,
    )
    own_rounded = own_weight.astype(jnp.bfloat16).astype(jnp.float32)
    weighted = weighted + own_rounded[..., None] * new_value.reshape(req_dev, kv_dev, 1, HD).astype(
        jnp.float32
    )
    local_out = weighted / weight_sum[..., None]
    local_log = running + jnp.log(weight_sum)
    prefix_out = prefix_out.reshape(req_dev, kv_dev, repeat, HD)
    prefix_log = prefix_log.reshape(req_dev, kv_dev, repeat)
    combined = jnp.logaddexp(prefix_log, local_log)
    attended = (
        prefix_out * jnp.exp(prefix_log - combined)[..., None]
        + local_out * jnp.exp(local_log - combined)[..., None]
    )
    attended = attended.reshape(req_dev, heads_dev * HD).astype(jnp.bfloat16)
    partial_value = jnp.dot(attended, o_weight, preferred_element_type=jnp.float32)
    proj = lax.psum(partial_value, "tp")
    summed = residual.astype(jnp.float32) + proj
    hidden = summed.astype(jnp.bfloat16)
    inverse = lax.rsqrt(jnp.mean(summed * summed, axis=-1, keepdims=True) + NORM_EPS)
    normed = (summed * inverse * norm_gain.astype(jnp.float32)[None, :]).astype(jnp.bfloat16)
    return (hidden, normed)


def solution(mesh):
    placed = (
        P("req", "tp"),
        P("req", "tp"),
        P("req", "tp"),
        P("req", None, "tp"),
        P("req", None, "tp"),
        P("req", None, "tp"),
        P("req", None, "tp"),
        P(),
        P("req"),
        P(),
        P("tp", None),
        P("req", None),
        P(),
    )
    return jax.shard_map(
        body,
        mesh=mesh,
        in_specs=placed,
        out_specs=(P("req", None), P("req", None)),
        check_vma=False,
    )
```

profile of v0, /device:TPU:2, one launch (start us, length us, event | category | flops | bytes accessed | tf_op | source)
XLA Modules:
  0.0 305.6 jit_solution(10688126659396240701)
XLA Ops:
  7.3 0.8 fusion.51
  8.2 0.8 broadcast_in_dim.180
  9.3 0.8 broadcast_in_dim.188
  10.5 0.7 fusion.59
  11.4 24.9 %all_gather.3 = bf16[768,512]{1,0:T(8,128)(2,1)S(1)} all-gather(bf16[24,512]{1,0:T(8,128)(2,1)} %param.15), channel_id=1, replica_groups=mesh['req'=32,'tp'=8] {'req'}, dimensions={0}, use_global_device_ids=true | all-gather | bytes 811008 | tf_op jit(solution)/shard_map/all_gather | solution.py:127
  36.8 50.0 %while.18 = (s32[]{:T(128)}, f32[64,1,4]{0,2,1:T(4,128)S(1)}, f32[64,1,4]{0,2,1:T(4,128)S(1)}, f32[64,1,4,128]{3,0,2,1:T(8,128)S(1)}, s32[2]{0:T(128)}, /*index=...) while((s32[]{:T(128)}, f32[64,1,4]{0,2,1:T(4,128)S(1)}, ...), condition=%wide.region_9.10_spmd.clone, body=%wide.region_6.9_spmd.clone.sunk | while | flops 136876160 | bytes 4351967 | solution.py:66
  37.0 0.7 broadcast_compare_fusion.5
  37.8 1.4 fusion.83
  39.6 1.4 fusion.86
  41.2 0.7 broadcast_compare_fusion.5
  42.0 1.4 fusion.83
  43.8 1.4 fusion.86
  45.3 0.7 broadcast_compare_fusion.5
  46.2 1.4 fusion.83
  47.9 1.4 fusion.86
  49.5 0.7 broadcast_compare_fusion.5
  50.3 1.4 fusion.83
  52.1 1.4 fusion.86
  53.7 0.7 broadcast_compare_fusion.5
  54.5 1.4 fusion.83
  56.3 1.4 fusion.86
  57.8 0.7 broadcast_compare_fusion.5
  58.7 1.4 fusion.83
  60.5 1.4 fusion.86
  62.0 0.7 broadcast_compare_fusion.5
  62.9 1.4 fusion.83
  64.6 1.4 fusion.86
  66.2 0.7 broadcast_compare_fusion.5
  67.0 1.4 fusion.83
  68.8 1.4 fusion.86
  70.3 0.7 broadcast_compare_fusion.5
  71.2 1.4 fusion.83
  73.0 1.4 fusion.86
  75.4 1.4 fusion.83
  77.1 1.4 fusion.86
  78.7 0.7 broadcast_compare_fusion.5
  79.5 1.4 fusion.83
  81.3 1.4 fusion.86
  83.7 1.4 fusion.83
  85.5 1.4 fusion.86
  87.2 2.0 fusion.27
  89.3 0.8 dynamic_slice.17
  91.6 109.0 %all-reduce = f32[768,4]{0,1:T(4,128)S(1)} all-reduce(f32[768,4]{0,1:T(4,128)S(1)} %fusion.26), channel_id=3, replica_groups=mesh['req'=32,'tp'=8] {'req'}, use_global_device_ids=true, to_apply=%region_11.12.clone | all-reduce | flops 3072 | bytes 24576
  201.9 0.8 reshape.377
  203.2 3.6 %fusion.37 = f32[24,4096]{1,0:T(8,128)} fusion(bf16[512,4096]{1,0:T(8,128)(2,1)} %param.25, bf16[3,8,4,128]{3,2,1,0:T(4,128)(2,1)S(1)} %bitcast.93), kind=kOutput, calls=%fused_computation.57 | convolution fusion | flops 100663296 | bytes 4612096 | tf_op jit(solution)/shard_map/dot_general | solution.py:186
  206.8 88.9 %all-reduce.3.cloned.1.call-done = f32[24,4096]{1,0:T(8,128)} async-done(((f32[24,4096]{1,0:T(8,128)}), f32[24,4096]{1,0:T(8,128)}) %all-reduce.3.cloned.1.call-update) | async-done | bytes 393232 | tf_op jit(solution)/shard_map/psum | solution.py:187
  295.8 1.2 multiply_reduce_fusion
  297.0 1.8 multiply_convert_fusion
  (177 shorter events, 13.2 us)
Async XLA Ops:
  7.2 193.8 %copy-start = (bf16[24,128,128]{2,1,0:T(8,128)(2,1)S(1)}, bf16[24,128,128]{2,1,0:T(8,128)(2,1)}, u32[]{:S(2)}) copy-start(bf16[24,128,128]{2,1,0:T(8,128)(2,1)} %param.20) | copy-start | bytes 2359300
  7.2 194.8 %reduce-scatter.3.cloned.1.call-start = ((), (), s32[]{:S(2)}) async-start(), calls=%async_computation.1 | async-start | bytes 1622016 | tf_op jit(solution)/shard_map/reduce_scatter | solution.py:139
  86.9 2.4 copy-start.2
  86.9 3.2 %copy-start.7 = (u32[256]{0:T(256)S(1)}, u32[256]{0:T(256)}, u32[]{:S(2)}) copy-start(u32[256]{0:T(256)} %constant.130) | copy-start | bytes 3076
  86.9 113.9 %copy-start.4 = (bf16[24,128]{1,0:T(8,128)(2,1)S(1)}, bf16[24,128]{1,0:T(8,128)(2,1)}, u32[]{:S(2)}) copy-start(bf16[24,128]{1,0:T(8,128)(2,1)} %param.17) | copy-start | bytes 18436
  86.9 113.9 %copy-start.6 = (bf16[24,128]{1,0:T(8,128)(2,1)S(1)}, bf16[24,128]{1,0:T(8,128)(2,1)}, u32[]{:S(2)}) copy-start(bf16[24,128]{1,0:T(8,128)(2,1)} %param.16) | copy-start | bytes 18436
  86.9 115.8 %copy-start.5 = (bf16[24,128,128]{2,1,0:T(8,128)(2,1)S(1)}, bf16[24,128,128]{2,1,0:T(8,128)(2,1)}, u32[]{:S(2)}) copy-start(bf16[24,128,128]{2,1,0:T(8,128)(2,1)} %param.21) | copy-start | bytes 2359300
  89.2 206.5 %all-reduce.3.cloned.1.call-start = ((), (), s32[]{:S(2)}) async-start(), calls=%async_computation.2 | async-start | bytes 786432 | tf_op jit(solution)/shard_map/psum | solution.py:187
  202.8 4.0 %copy-start.3 = (bf16[4096]{0:T(1024)(128)(2,1)S(1)}, bf16[4096]{0:T(1024)(128)(2,1)}, u32[]{:S(2)}) copy-start(bf16[4096]{0:T(1024)(128)(2,1)} %param.27) | copy-start | bytes 24580
  202.8 93.0 %copy-start.1 = (bf16[24,4096]{1,0:T(8,128)(2,1)S(1)}, bf16[24,4096]{1,0:T(8,128)(2,1)}, u32[]{:S(2)}) copy-start(bf16[24,4096]{1,0:T(8,128)(2,1)} %param.26) | copy-start | bytes 589828
Sparse Core Ops, SparseCore 0:
  89.4 86.8 reduce-scatter.2
  206.9 88.8 all-reduce.2
where the time goes:
time: 307 us; the launch traced here: 306 us
  blocking collectives  134 us (44%)
  waiting for transfers between devices  89 us (29%)
  matrix products  40.4 us (13%)
  other arithmetic  21.3 us (7%)
  between operations  15 us (5%)
  local copies, waits for them, and re-layouts  5.04 us (2%)
    unnamed x1, blocking collectives  109 us
    psum x1, waiting for transfers between devices, body(): proj = lax.psum(partial_value, 'tp')  88.9 us
    all_gather x1, blocking collectives, body(): every_query = lax.all_gather(query, 'req', axis=0, tiled=True)  24.9 us
    dot_general x12, matrix products, key_step(): jnp.einsum('rkhgp,gpkd->rkhd', rounded, value_block, preferred_element_ty...  16.8 us
    dot_general x12, matrix products, key_step(): jnp.einsum('rkhd,gpkd->rkhgp', queries, key_block, preferred_element_type...  16.3 us
    lt x12, other arithmetic, key_step(): inside = positions[None, :] < prompt_len[:, None]  8.77 us
  transfers between devices with their start and end apart: 2, of which 1 were waited for; matrix products, arithmetic and copies ran while one was open for 1% of the time, Pallas kernels for 0%

commit v1 on v0

--- a/solution.py
+++ b/solution.py
@@ -124,7 +124,9 @@
     slot_row = jnp.where(filled, jnp.sum(jnp.where(slot_pick, all_rows, 0), axis=2), -1).reshape(
         slot_total
     )
-    every_query = lax.all_gather(query, "req", axis=0, tiled=True)
+    every_query = jnp.concatenate(
+        lax.all_to_all(jnp.stack([query] * lax.axis_size("req")), "req", 0, 0), axis=0
+    )
     pick_rows = slot_row[:, None] == jnp.arange(places * req_dev, dtype=jnp.int32)[None, :]
     compact = jnp.dot(
         pick_rows.astype(jnp.bfloat16), every_query, preferred_element_type=jnp.float32

time: 307 us -> 292 us (0.951)
  blocking collectives: 134 us -> 110 us
  other arithmetic: 21.3 us -> 13.3 us
  waiting for transfers between devices: 89 us -> 96.8 us
  starting transfers between devices: 0.08 us -> 7.7 us
    all_gather x1 -> x0, blocking collectives: 24.9 us -> none  [body(): every_query = lax.all_gather(query, 'req', axis=0, tiled=True)]
    lt x12, other arithmetic: 8.77 us -> 0.89 us  [key_step(): inside = positions[None, :] < prompt_len[:, None]]
    all_to_all x0 -> x1, waiting for transfers between devices: none -> 7.68 us  [body(): lax.all_to_all(jnp.stack([query] * lax.axis_size('req')), 'req', 0, 0)]
    all_to_all x0 -> x1, starting transfers between devices: none -> 7.62 us  [body(): lax.all_to_all(jnp.stack([query] * lax.axis_size('req')), 'req', 0, 0)]
  transfers between devices with their start and end apart: 2 -> 3, of which waited for: 1 -> 2; matrix products, arithmetic and copies ran while one was open for 1% -> 2% of each run, Pallas kernels for 0% -> 0%
where the time goes in v1:
time: 292 us; the launch traced here: 291 us
  blocking collectives  110 us (38%)
  waiting for transfers between devices  96.8 us (33%)
  matrix products  40.4 us (14%)
  between operations  15 us (5%)
  other arithmetic  13.3 us (5%)
  starting transfers between devices  7.7 us (3%)
  local copies, waits for them, and re-layouts  6.8 us (2%)
    unnamed x1, blocking collectives  110 us
    psum x1, waiting for transfers between devices, body(): proj = lax.psum(partial_value, 'tp')  89.1 us
    dot_general x12, matrix products, key_step(): jnp.einsum('rkhgp,gpkd->rkhd', rounded, value_block, preferred_element_ty...  16.8 us
    dot_general x12, matrix products, key_step(): jnp.einsum('rkhd,gpkd->rkhgp', queries, key_block, preferred_element_type...  16.3 us
    all_to_all x1, waiting for transfers between devices, body(): lax.all_to_all(jnp.stack([query] * lax.axis_size('req')), 'req', 0, 0)  7.68 us
    all_to_all x1, starting transfers between devices, body(): lax.all_to_all(jnp.stack([query] * lax.axis_size('req')), 'req', 0, 0)  7.62 us
  transfers between devices with their start and end apart: 3, of which 2 were waited for; matrix products, arithmetic and copies ran while one was open for 2% of the time, Pallas kernels for 0%

profile of v1, /device:TPU:2, one launch (start us, length us, event | category | flops | bytes accessed | tf_op | source)
XLA Modules:
  0.0 290.8 jit_solution(12943070124509745079)
XLA Ops:
  7.2 1.7 stack.2
  8.9 7.6 %all-to-all-start = ((bf16[32,24,512]{2,1,0:T(8,128)(2,1)}), bf16[32,24,512]{2,1,0:T(8,128)(2,1)S(1)}, u32[]{:S(2)}, u32[]{:S(2)}) async-start(bf16[32,24,512]{2,1,0:T(8,128)(2,1)} %stack.2), calls=%async_computation | async-start | bytes 1572864 | tf_op jit(solution)/shard_map/all_to_all | solution.py:128
  16.6 0.7 fusion.51
  17.5 0.8 broadcast_in_dim.180
  18.6 0.8 broadcast_in_dim.188
  20.2 0.7 fusion.59
  20.9 7.7 %all-to-all-done = bf16[32,24,512]{2,1,0:T(8,128)(2,1)S(1)} async-done(((bf16[32,24,512]{2,1,0:T(8,128)(2,1)}), bf16[32,24,512]{2,1,0:T(8,128)(2,1)S(1)}, u32[]{:S(2)}, u32[]{:S(2)}) %all-to-all-start) | async-done | bytes 786464 | tf_op jit(solution)/shard_map/all_to_all | solution.py:128
  29.0 42.2 %while.18 = (s32[]{:T(128)}, f32[64,1,4]{0,2,1:T(4,128)S(1)}, f32[64,1,4]{0,2,1:T(4,128)S(1)}, f32[64,1,4,128]{3,0,2,1:T(8,128)S(1)}, s32[2]{0:T(128)S(1)}, /*in...) while((s32[]{:T(128)}, f32[64,1,4]{0,2,1:T(4,128)S(1)}, ...), condition=%wide.region_9.10_spmd.clone, body=%wide.region_6.9_spmd.clone.sunk | while | flops 136876160 | bytes 4351967 | solution.py:66
  29.3 1.4 fusion.83
  30.7 0.4 fusion.85
  31.1 1.4 fusion.86
  32.8 1.4 fusion.83
  34.2 0.4 fusion.85
  34.6 1.4 fusion.86
  36.3 1.4 fusion.83
  37.7 0.4 fusion.85
  38.1 1.4 fusion.86
  39.9 1.4 fusion.83
  41.2 0.4 fusion.85
  41.6 1.4 fusion.86
  43.4 1.4 fusion.83
  44.8 0.4 fusion.85
  45.1 1.4 fusion.86
  46.9 1.4 fusion.83
  48.7 1.4 fusion.86
  50.4 1.4 fusion.83
  52.2 1.4 fusion.86
  53.9 1.4 fusion.83
  55.7 1.4 fusion.86
  57.4 1.4 fusion.83
  59.2 1.4 fusion.86
  60.9 1.4 fusion.83
  62.7 1.4 fusion.86
  64.5 1.4 fusion.83
  66.2 1.4 fusion.86
  68.0 1.4 fusion.83
  69.7 1.4 fusion.86
  71.4 2.0 fusion.27
  73.6 0.8 dynamic_slice.17
  74.4 0.6 dynamic-slice
  75.8 0.6 fusion.68
  76.9 109.8 %all-reduce = f32[768,4]{0,1:T(4,128)S(1)} all-reduce(f32[768,4]{0,1:T(4,128)S(1)} %fusion.26), channel_id=3, replica_groups=mesh['req'=32,'tp'=8] {'req'}, use_global_device_ids=true, to_apply=%region_11.12.clone | all-reduce | flops 3072 | bytes 24576
  187.0 0.8 reshape.383
  187.8 0.4 fusion.25
  188.2 3.6 %fusion.37 = f32[24,4096]{1,0:T(8,128)} fusion(bf16[512,4096]{1,0:T(8,128)(2,1)} %param.25, bf16[3,8,4,128]{3,2,1,0:T(4,128)(2,1)S(1)} %bitcast.95), kind=kOutput, calls=%fused_computation.57 | convolution fusion | flops 100663296 | bytes 4612096 | tf_op jit(solution)/shard_map/dot_general | solution.py:188
  191.9 89.1 %all-reduce.3.cloned.1.call-done = f32[24,4096]{1,0:T(8,128)} async-done(((f32[24,4096]{1,0:T(8,128)}), f32[24,4096]{1,0:T(8,128)}) %all-reduce.3.cloned.1.call-update) | async-done | bytes 393232 | tf_op jit(solution)/shard_map/psum | solution.py:189
  281.0 1.2 multiply_reduce_fusion
  282.1 1.8 multiply_convert_fusion
  (181 shorter events, 9.2 us)
Async XLA Ops:
  7.2 68.7 %copy-start = (bf16[24,128,128]{2,1,0:T(8,128)(2,1)S(1)}, bf16[24,128,128]{2,1,0:T(8,128)(2,1)}, u32[]{:S(2)}) copy-start(bf16[24,128,128]{2,1,0:T(8,128)(2,1)} %param.20) | copy-start | bytes 2359300
  7.2 21.8 %copy-start.3 = (s32[2]{0:T(128)S(1)}, s32[2]{0:T(128)}, u32[]{:S(2)}) copy-start(s32[2]{0:T(128)} %param.23) | copy-start | bytes 28
  8.9 19.7 %all-to-all-start = ((bf16[32,24,512]{2,1,0:T(8,128)(2,1)}), bf16[32,24,512]{2,1,0:T(8,128)(2,1)S(1)}, u32[]{:S(2)}, u32[]{:S(2)}) async-start(bf16[32,24,512]{2,1,0:T(8,128)(2,1)} %stack.2), calls=%async_computation | async-start | bytes 1572864 | tf_op jit(solution)/shard_map/all_to_all | solution.py:128
  16.6 170.4 %reduce-scatter.3.cloned.1.call-start = ((), (), s32[]{:S(2)}) async-start(), calls=%async_computation.2 | async-start | bytes 1622016 | tf_op jit(solution)/shard_map/reduce_scatter | solution.py:141
  71.2 2.4 copy-start.2
  71.2 3.2 %copy-start.5 = (bf16[24,128]{1,0:T(8,128)(2,1)S(1)}, bf16[24,128]{1,0:T(8,128)(2,1)}, u32[]{:S(2)}) copy-start(bf16[24,128]{1,0:T(8,128)(2,1)} %param.17) | copy-start | bytes 18436
  71.2 3.2 %copy-start.8 = (u32[256]{0:T(256)S(1)}, u32[256]{0:T(256)}, u32[]{:S(2)}) copy-start(u32[256]{0:T(256)} %constant.130) | copy-start | bytes 3076
  71.2 4.5 %copy-start.7 = (bf16[24,128]{1,0:T(8,128)(2,1)S(1)}, bf16[24,128]{1,0:T(8,128)(2,1)}, u32[]{:S(2)}) copy-start(bf16[24,128]{1,0:T(8,128)(2,1)} %param.16) | copy-start | bytes 18436
  71.2 116.6 %copy-start.6 = (bf16[24,128,128]{2,1,0:T(8,128)(2,1)S(1)}, bf16[24,128,128]{2,1,0:T(8,128)(2,1)}, u32[]{:S(2)}) copy-start(bf16[24,128,128]{2,1,0:T(8,128)(2,1)} %param.21) | copy-start | bytes 2359300
  73.5 207.4 %all-reduce.3.cloned.1.call-start = ((), (), s32[]{:S(2)}) async-start(), calls=%async_computation.3 | async-start | bytes 786432 | tf_op jit(solution)/shard_map/psum | solution.py:189
  187.8 4.0 %copy-start.4 = (bf16[4096]{0:T(1024)(128)(2,1)S(1)}, bf16[4096]{0:T(1024)(128)(2,1)}, u32[]{:S(2)}) copy-start(bf16[4096]{0:T(1024)(128)(2,1)} %param.27) | copy-start | bytes 24580
  187.8 93.1 %copy-start.1 = (bf16[24,4096]{1,0:T(8,128)(2,1)S(1)}, bf16[24,4096]{1,0:T(8,128)(2,1)}, u32[]{:S(2)}) copy-start(bf16[24,4096]{1,0:T(8,128)(2,1)} %param.26) | copy-start | bytes 589828
Sparse Core Ops, SparseCore 0:
  73.6 87.0 reduce-scatter.2
  192.0 88.9 all-reduce.2
